TPU v7x, 128 devices: a whole 4x4x4 slice. The times are simulated.
128 devices in a mesh: dp: 2 (over core), cent: 64 (over z, y, x).
Axes of the slice: x: 4, y: 4, z: 4, core: 2. Of those that a mesh axis runs over, the one named last changes fastest.
Arguments:
- points: bfloat16 [16384, 768], P(('dp', 'cent')), may hold values from -16 to 16
- centroids: float32 [32768, 768], P(('dp', 'cent')), may hold values from -1.5 to 1.5
Outputs:
- new_centroids: float32 [32768, 768], P(('dp', 'cent'))
- log_total: float32 [16384], P(('dp', 'cent'))
All inputs are finite; a program needn't handle non-finite values.
Results may differ from a plain program's by a relative error of at most 0.0088.
Values may be sent and summed in bfloat16 or wider, within the bound.
No kernel may reach another device: no remote copies, remote signals or barrier semaphores. Data moves between devices by JAX's collectives and lax.ppermute only.
A program may use at most 128 MiB of HBM per device.

v0:
```python
import math
import jax
import jax.numpy as jnp
from jax import lax
from jax.sharding import PartitionSpec as P

HALVES = 2


def score_block(members, cent_block, score_scale):
    sq_norm = jnp.sum(jnp.square(cent_block.astype(jnp.float32)), axis=1)
    products = lax.dot_general(
        members, cent_block, (((1,), (1,)), ((), ())), preferred_element_type=jnp.float32
    )
    return (2.0 * products - sq_norm[None, :]) * score_scale


def group_log_total(local_max, local_sum, own_points):
    cent_count = lax.axis_size("cent")
    packed = jnp.stack(
        [local_max.reshape(cent_count, own_points), local_sum.reshape(cent_count, own_points)],
        axis=1,
    )
    parts = lax.all_to_all(packed, "cent", 0, 0, tiled=True)
    part_max, part_sum = (parts[:, 0], parts[:, 1])
    top = jnp.max(part_max, axis=0)
    total = jnp.sum(part_sum * jnp.exp(part_max - top[None, :]), axis=0)
    own_total = top + jnp.log(total)
    spread = jnp.broadcast_to(own_total[None], (cent_count, own_points))
    log_total = lax.all_to_all(spread, "cent", 0, 0, tiled=True).reshape(cent_count * own_points)
    return (own_total, log_total)


def on_device(points, centroids):
    feature_width = centroids.shape[1]
    own_points = points.shape[0]
    cent_count = lax.axis_size("cent")
    score_scale = 7.0 / math.sqrt(feature_width)
    copies = centroids.astype(jnp.bfloat16)
    members = lax.all_gather(points, "cent", axis=0, tiled=True)
    gathered = lax.all_gather(copies, "dp", axis=0, tiled=True)
    half_points = own_points // HALVES
    split = members.reshape(cent_count, HALVES, half_points, feature_width)
    own_parts = []
    sums = None
    counts = None
    for index_h in range(HALVES):
        half = split[:, index_h].reshape(cent_count * half_points, feature_width)
        scores = score_block(half, gathered, score_scale)
        local_max = jnp.max(scores, axis=1)
        local_sum = jnp.sum(jnp.exp(scores - local_max[:, None]), axis=1)
        own_total, log_total = group_log_total(local_max, local_sum, half_points)
        own_parts.append(own_total)
        weights = jnp.exp(scores - log_total[:, None]).astype(jnp.bfloat16)
        part_sums = lax.dot_general(
            weights, half, (((0,), (0,)), ((), ())), preferred_element_type=jnp.float32
        )
        part_counts = jnp.sum(weights, axis=0, dtype=jnp.float32)
        sums = part_sums if sums is None else sums + part_sums
        counts = part_counts if counts is None else counts + part_counts
    own_sums = lax.psum_scatter(sums, "dp", scatter_dimension=0, tiled=True)
    own_counts = lax.psum_scatter(counts, "dp", scatter_dimension=0, tiled=True)
    new_centroids = (own_sums + centroids) / (own_counts[:, None] + 1.0)
    return (new_centroids, jnp.concatenate(own_parts))


def solution(mesh):
    placed = (P(("dp", "cent"), None), P(("dp", "cent"), None))
    return jax.shard_map(
        on_device,
        mesh=mesh,
        in_specs=placed,
        out_specs=(P(("dp", "cent"), None), P(("dp", "cent"))),
        check_vma=False,
    )
```

profile of v0, /device:TPU:1, one launch (start us, length us, event | category | flops | bytes accessed | tf_op | source)
XLA Modules:
  0.0 230.5 jit_solution(3304867153175038017)
XLA Ops:
  7.9 1.2 convert_element_type.19
  9.1 3.4 %all_gather.7 = bf16[512,768]{1,0:T(8,128)(2,1)S(1)} all-gather(bf16[256,768]{1,0:T(8,128)(2,1)S(1)} %convert_element_type.19), channel_id=1, replica_groups=mesh['dp'=2,'cent'=64] {'dp'}, dimensions={0}, use_global_device_ids=true | all-gather | bytes 1179648 | tf_op jit(solution)/shard_map/all_gather | solution.py:41
  12.7 92.0 %all-gather.2.cloned.1.call-done = bf16[8192,768]{1,0:T(8,128)(2,1)} async-done(((bf16[128,768]{1,0:T(8,128)(2,1)}), bf16[8192,768]{1,0:T(8,128)(2,1)}) %all-gather.2.cloned.1.call-update) | async-done | bytes 12582928 | tf_op jit(solution)/shard_map/all_gather | solution.py:40
  104.7 8.6 %fusion.1 = (bf16[64,1,64,768]{3,2,1,0:T(8,128)(2,1)}, bf16[64,1,64,768]{3,2,1,0:T(8,128)(2,1)S(1)}) fusion(bf16[64,2,64,768]{3,2,1,0:T(8,128)(2,1)} %bitcast.18), kind=kLoop, calls=%fused_computation.20 | loop fusion | bytes 25165824 | tf_op jit(solution)/shard_map/slice | solution.py:48
  113.4 5.8 %fusion.4 = (f32[4096]{0:T(1024)S(1)}, f32[4096,512]{0,1:T(8,128)}) fusion(f32[512]{0:T(512)S(1)} %multiply_reduce_fusion, bf16[4096,768]{1,0:T(8,128)(2,1)S(1)} %bitcast.21, bf16[512,768]{1,0:T(8,128)(2,1)S(1)} %all_gather.7), kind=kOutput, calls=%fused_computation.23 | convolution fusion | flops 3229609984 | bytes 15484928 | tf_op jit(solution)/shard_map/dot_general | solution.py:12
  119.2 4.5 %exponential_reduce_fusion.1 = f32[4096]{0:T(1024)S(1)} fusion(f32[4096,512]{0,1:T(8,128)} %get-tuple-element.9, f32[4096]{0:T(1024)S(1)} %get-tuple-element.8), kind=kLoop, calls=%fused_computation.6 | loop fusion | flops 4190208 | bytes 8421376 | tf_op jit(solution)/shard_map/reduce_sum | solution.py:51
  123.9 0.7 reshape.60
  124.7 8.3 %all-to-all-start = ((f32[64,1,128]{2,1,0:T(1,128)}), f32[64,1,128]{2,1,0:T(1,128)S(1)}, u32[]{:S(2)}, u32[]{:S(2)}) async-start(f32[64,1,128]{2,1,0:T(1,128)} %reshape.60), calls=%async_computation | async-start | bytes 65536 | tf_op jit(solution)/shard_map/all_to_all | solution.py:24
  133.0 8.5 %fusion.5 = (f32[4096]{0:T(1024)S(1)}, f32[4096,512]{0,1:T(8,128)}) fusion(f32[512]{0:T(512)S(1)} %multiply_reduce_fusion, bf16[4096,768]{1,0:T(8,128)(2,1)} %bitcast.19, bf16[512,768]{1,0:T(8,128)(2,1)S(1)} %all_gather.7), kind=kOutput, calls=%fused_computation.24 | convolution fusion | flops 3229609984 | bytes 15484928 | tf_op jit(solution)/shard_map/dot_general | solution.py:12
  141.6 4.5 %exponential_reduce_fusion = f32[4096]{0:T(1024)S(1)} fusion(f32[4096,512]{0,1:T(8,128)} %get-tuple-element.11, f32[4096]{0:T(1024)S(1)} %get-tuple-element.10), kind=kLoop, calls=%fused_computation.3 | loop fusion | flops 4190208 | bytes 8421376 | tf_op jit(solution)/shard_map/reduce_sum | solution.py:51
  147.0 9.8 %all-to-all-start.2 = ((f32[64,1,128]{2,1,0:T(1,128)}), f32[64,1,128]{2,1,0:T(1,128)S(1)}, u32[]{:S(2)}, u32[]{:S(2)}) async-start(f32[64,1,128]{2,1,0:T(1,128)} %reshape.62), calls=%async_computation.2 | async-start | bytes 65536 | tf_op jit(solution)/shard_map/all_to_all | solution.py:24
  158.3 7.0 %all-to-all-done.2 = f32[64,1,128]{2,1,0:T(1,128)S(1)} async-done(((f32[64,1,128]{2,1,0:T(1,128)}), f32[64,1,128]{2,1,0:T(1,128)S(1)}, u32[]{:S(2)}, u32[]{:S(2)}) %all-to-all-start.2) | async-done | bytes 32800 | tf_op jit(solution)/shard_map/all_to_all | solution.py:24
  165.8 4.7 %all-to-all-start.1 = ((f32[64,1,64]{2,1,0:T(1,128)}), f32[64,1,64]{2,1,0:T(1,128)S(1)}, u32[]{:S(2)}, u32[]{:S(2)}) async-start(f32[64,1,64]{2,1,0:T(1,128)} %broadcast_in_dim.4), calls=%async_computation.1 | async-start | bytes 65536 | tf_op jit(solution)/shard_map/all_to_all | solution.py:30
  170.5 0.7 reduce.11
  171.5 7.4 %all-to-all-done.1 = f32[64,1,64]{2,1,0:T(1,128)S(1)} async-done(((f32[64,1,64]{2,1,0:T(1,128)}), f32[64,1,64]{2,1,0:T(1,128)S(1)}, u32[]{:S(2)}, u32[]{:S(2)}) %all-to-all-start.1) | async-done | bytes 16416 | tf_op jit(solution)/shard_map/all_to_all | solution.py:30
  179.5 4.7 %all-to-all-start.3 = ((f32[64,1,64]{2,1,0:T(1,128)}), f32[64,1,64]{2,1,0:T(1,128)S(1)}, u32[]{:S(2)}, u32[]{:S(2)}) async-start(f32[64,1,64]{2,1,0:T(1,128)} %broadcast_in_dim.5), calls=%async_computation.3 | async-start | bytes 65536 | tf_op jit(solution)/shard_map/all_to_all | solution.py:30
  185.0 0.7 reduce.8
  185.8 7.7 %fusion = f32[512,768]{1,0:T(8,128)S(1)} fusion(bf16[4096,768]{1,0:T(8,128)(2,1)} %bitcast.22, f32[4096,512]{0,1:T(8,128)} %get-tuple-element.9, f32[4096]{0:T(1024)S(1)} %sub.72), kind=kOutput, calls=%fused_computation.10 | convolution fusion | flops 3225419776 | bytes 16269312 | tf_op jit(solution)/shard_map/dot_general | solution.py:55
  193.5 0.7 reduce.9
  194.3 9.8 %convolution_add_fusion = f32[512,768]{1,0:T(8,128)} fusion(f32[512,768]{1,0:T(8,128)S(1)} %fusion, bf16[4096,768]{1,0:T(8,128)(2,1)} %bitcast.20, f32[4096,512]{0,1:T(8,128)} %get-tuple-element.11, f32[4096]{0:T(1024)S(1)} %sub.80), kind=kOutput, calls=%fused_computation.9 | convolution fusion | flops 3225812992 | bytes 17842176 | tf_op jit(solution)/shard_map/dot_general | solution.py:55
  205.9 7.1 %convert_reduce_fusion = (f32[512]{0:T(512)S(1)}, f32[512]{0:T(512)S(1)}) fusion(f32[4096,512]{0,1:T(8,128)} %get-tuple-element.11, f32[4096]{0:T(1024)S(1)} %sub.80, f32[4096,512]{0,1:T(8,128)} %get-tuple-element.9, f32[4096]{0:T(1024)S(1)} %sub.72), kind=kLoop, calls=%fused_computation | loop fusion | flops 16776192 | bytes 16814080 | tf_op jit(solution)/shard_map/reduce_sum | solution.py:58
  213.1 6.9 %all-reduce = f32[512]{0:T(512)S(1)} all-reduce(f32[512]{0:T(512)S(1)} %add.38), channel_id=3, replica_groups=mesh['dp'=2,'cent'=64] {'dp'}, use_global_device_ids=true, to_apply=%region_12.0.clone | all-reduce | flops 512 | bytes 4096
  220.0 1.4 reduce-scatter.2.cloned.1.call-done
  221.5 2.1 add_divide_fusion
  (41 shorter events, 7.3 us)
Async XLA Ops:
  7.2 97.6 %all-gather.2.cloned.1.call-start = ((), (), s32[]{:S(2)}) async-start(), calls=%async_computation.5 | async-start | bytes 12779520 | tf_op jit(solution)/shard_map/all_gather | solution.py:40
  113.4 5.8 %copy-start = (bf16[64,1,64,768]{3,2,1,0:T(8,128)(2,1)}, bf16[64,1,64,768]{3,2,1,0:T(8,128)(2,1)S(1)}, u32[]{:S(2)}) copy-start(bf16[64,1,64,768]{3,2,1,0:T(8,128)(2,1)S(1)} %get-tuple-element.3) | copy-start | bytes 18874372
  124.7 22.3 %all-to-all-start = ((f32[64,1,128]{2,1,0:T(1,128)}), f32[64,1,128]{2,1,0:T(1,128)S(1)}, u32[]{:S(2)}, u32[]{:S(2)}) async-start(f32[64,1,128]{2,1,0:T(1,128)} %reshape.60), calls=%async_computation | async-start | bytes 65536 | tf_op jit(solution)/shard_map/all_to_all | solution.py:24
  147.0 18.2 %all-to-all-start.2 = ((f32[64,1,128]{2,1,0:T(1,128)}), f32[64,1,128]{2,1,0:T(1,128)S(1)}, u32[]{:S(2)}, u32[]{:S(2)}) async-start(f32[64,1,128]{2,1,0:T(1,128)} %reshape.62), calls=%async_computation.2 | async-start | bytes 65536 | tf_op jit(solution)/shard_map/all_to_all | solution.py:24
  165.8 13.0 %all-to-all-start.1 = ((f32[64,1,64]{2,1,0:T(1,128)}), f32[64,1,64]{2,1,0:T(1,128)S(1)}, u32[]{:S(2)}, u32[]{:S(2)}) async-start(f32[64,1,64]{2,1,0:T(1,128)} %broadcast_in_dim.4), calls=%async_computation.1 | async-start | bytes 65536 | tf_op jit(solution)/shard_map/all_to_all | solution.py:30
  179.5 14.0 %all-to-all-start.3 = ((f32[64,1,64]{2,1,0:T(1,128)}), f32[64,1,64]{2,1,0:T(1,128)S(1)}, u32[]{:S(2)}, u32[]{:S(2)}) async-start(f32[64,1,64]{2,1,0:T(1,128)} %broadcast_in_dim.5), calls=%async_computation.3 | async-start | bytes 65536 | tf_op jit(solution)/shard_map/all_to_all | solution.py:30
  184.2 37.3 %reduce-scatter.2.cloned.1.call-start = ((), (), s32[]{:S(2)}) async-start(), calls=%async_computation.6 | async-start | bytes 2359296 | tf_op jit(solution)/shard_map/reduce_scatter | solution.py:61
  194.3 9.8 %copy-start.2 = (u32[128]{0:T(128)S(1)}, u32[128]{0:T(128)}, u32[]{:S(2)}) copy-start(u32[128]{0:T(128)} %constant.12) | copy-start | bytes 1540
  205.9 15.5 %copy-start.1 = (f32[256,768]{1,0:T(8,128)S(1)}, f32[256,768]{1,0:T(8,128)}, u32[]{:S(2)}) copy-start(f32[256,768]{1,0:T(8,128)} %param.3) | copy-start | bytes 2359300
Sparse Core Ops, SparseCore 0:
  10.7 93.9 all-gather.1
  204.2 17.1 reduce-scatter.1
where the time goes:
time: 231 us; the launch traced here: 230 us
  waiting for transfers between devices  109 us (47%)
  matrix products  31.7 us (14%)
  starting transfers between devices  27.7 us (12%)
  other arithmetic  23.6 us (10%)
  between operations  14.9 us (6%)
  local copies, waits for them, and re-layouts  13.8 us (6%)
  blocking collectives  10.2 us (4%)
    all_gather x1, waiting for transfers between devices, on_device(): members = lax.all_gather(points, 'cent', axis=0, tiled=True)  92 us
    all_to_all x2, starting transfers between devices, group_log_total(): parts = lax.all_to_all(packed, 'cent', 0, 0, tiled=True)  18.1 us
    dot_general x2, matrix products, on_device(): lax.dot_general(weights, half, (((0,), (0,)), ((), ())), preferred_elemen...  17.5 us
    dot_general x2, matrix products, score_block(): lax.dot_general(members, cent_block, (((1,), (1,)), ((), ())), preferred_...  14.2 us
    all_to_all x2, starting transfers between devices, group_log_total(): lax.all_to_all(spread, 'cent', 0, 0, tiled=True)  9.36 us
    reduce_sum x2, other arithmetic, on_device(): local_sum = jnp.sum(jnp.exp(scores - local_max[:, None]), axis=1)  9.06 us
    slice x1, local copies, waits for them, and re-layouts, on_device(): half = split[:, index_h].reshape(cent_count * half_points, feature_width)  8.65 us
    all_to_all x2, waiting for transfers between devices, group_log_total(): lax.all_to_all(spread, 'cent', 0, 0, tiled=True)  7.39 us
  transfers between devices with their start and end apart: 6, of which 4 were waited for; matrix products, arithmetic and copies ran while one was open for 15% of the time, Pallas kernels for 0%

commit v1 on v0

--- a/solution.py
+++ b/solution.py
@@ -37,7 +37,10 @@
     cent_count = lax.axis_size("cent")
     score_scale = 7.0 / math.sqrt(feature_width)
     copies = centroids.astype(jnp.bfloat16)
-    members = lax.all_gather(points, "cent", axis=0, tiled=True)
+    peers = lax.axis_size("cent")
+    shards = jnp.stack([points for _ in range(peers)])
+    shards = lax.all_to_all(shards, "cent", split_axis=0, concat_axis=0)
+    members = jnp.concatenate(shards, axis=0)
     gathered = lax.all_gather(copies, "dp", axis=0, tiled=True)
     half_points = own_points // HALVES
     split = members.reshape(cent_count, HALVES, half_points, feature_width)

time: 231 us -> 357 us (1.55)
  waiting for transfers between devices: 109 us -> 215 us
  starting transfers between devices: 27.7 us -> 40.7 us
  local copies, waits for them, and re-layouts: 13.8 us -> 20.7 us
    all_to_all x0 -> x1, waiting for transfers between devices: none -> 200 us  [on_device(): shards = lax.all_to_all(shards, 'cent', split_axis=0, concat_axis=0)]
    all_gather x1 -> x0, waiting for transfers between devices: 92 us -> none  [on_device(): members = lax.all_gather(points, 'cent', axis=0, tiled=True)]
    all_to_all x0 -> x1, starting transfers between devices: none -> 12.3 us  [on_device(): shards = lax.all_to_all(shards, 'cent', split_axis=0, concat_axis=0)]
    another operation x0 -> x1, local copies, waits for them, and re-layouts: none -> 6.92 us  [on_device(): shards = jnp.stack([points for _ in range(peers)])]
  transfers between devices with their start and end apart: 6 -> 6, of which waited for: 4 -> 4; matrix products, arithmetic and copies ran while one was open for 15% -> 10% of each run, Pallas kernels for 0% -> 0%
where the time goes in v1:
time: 357 us; the launch traced here: 356 us
  waiting for transfers between devices  215 us (60%)
  starting transfers between devices  40.7 us (11%)
  matrix products  31.7 us (9%)
  other arithmetic  22.4 us (6%)
  local copies, waits for them, and re-layouts  20.7 us (6%)
  between operations  14.9 us (4%)
  blocking collectives  10.7 us (3%)
    all_to_all x1, waiting for transfers between devices, on_device(): shards = lax.all_to_all(shards, 'cent', split_axis=0, concat_axis=0)  200 us
    all_to_all x2, starting transfers between devices, group_log_total(): parts = lax.all_to_all(packed, 'cent', 0, 0, tiled=True)  18.8 us
    dot_general x2, matrix products, on_device(): lax.dot_general(weights, half, (((0,), (0,)), ((), ())), preferred_elemen...  17.5 us
    dot_general x2, matrix products, score_block(): lax.dot_general(members, cent_block, (((1,), (1,)), ((), ())), preferred_...  14.2 us
    all_to_all x1, starting transfers between devices, on_device(): shards = lax.all_to_all(shards, 'cent', split_axis=0, concat_axis=0)  12.3 us
    all_to_all x2, starting transfers between devices, group_log_total(): lax.all_to_all(spread, 'cent', 0, 0, tiled=True)  9.54 us
    reduce_sum x2, other arithmetic, on_device(): local_sum = jnp.sum(jnp.exp(scores - local_max[:, None]), axis=1)  9.06 us
    slice x1, local copies, waits for them, and re-layouts, on_device(): half = split[:, index_h].reshape(cent_count * half_points, feature_width)  8.65 us
  transfers between devices with their start and end apart: 6, of which 4 were waited for; matrix products, arithmetic and copies ran while one was open for 10% of the time, Pallas kernels for 0%

profile of v1, /device:TPU:1, one launch (start us, length us, event | category | flops | bytes accessed | tf_op | source)
XLA Modules:
  0.0 356.2 jit_solution(14049078837834875513)
XLA Ops:
  7.2 6.9 %stack.6 = bf16[64,128,768]{2,1,0:T(8,128)(2,1)} broadcast(bf16[128,768]{1,0:T(8,128)(2,1)} %param.2), dimensions={1,2} | broadcast | bytes 12779520 | tf_op jit(solution)/shard_map/stack | solution.py:41
  14.1 12.3 %all-to-all-start = ((bf16[64,128,768]{2,1,0:T(8,128)(2,1)}), bf16[64,128,768]{2,1,0:T(8,128)(2,1)}, u32[]{:S(2)}, u32[]{:S(2)}) async-start(bf16[64,128,768]{2,1,0:T(8,128)(2,1)} %stack.6), calls=%async_computation | async-start | bytes 25165824 | tf_op jit(solution)/shard_map/all_to_all | solution.py:42
  26.5 3.0 all_gather.3
  29.6 199.5 %all-to-all-done = bf16[64,128,768]{2,1,0:T(8,128)(2,1)} async-done(((bf16[64,128,768]{2,1,0:T(8,128)(2,1)}), bf16[64,128,768]{2,1,0:T(8,128)(2,1)}, u32[]{:S(2)}, u32[]{:S(2)}) %all-to-all-start) | async-done | bytes 12582944 | tf_op jit(solution)/shard_map/all_to_all | solution.py:42
  229.2 8.6 %fusion.1 = (bf16[64,1,64,768]{3,2,1,0:T(8,128)(2,1)}, bf16[64,1,64,768]{3,2,1,0:T(8,128)(2,1)S(1)}) fusion(bf16[64,2,64,768]{3,2,1,0:T(8,128)(2,1)} %bitcast), kind=kLoop, calls=%fused_computation.20 | loop fusion | bytes 25165824 | tf_op jit(solution)/shard_map/slice | solution.py:51
  237.8 5.8 %fusion.4 = (f32[4096]{0:T(1024)S(1)}, f32[4096,512]{0,1:T(8,128)}) fusion(f32[512]{0:T(512)S(1)} %multiply_reduce_fusion, bf16[4096,768]{1,0:T(8,128)(2,1)S(1)} %bitcast.20, bf16[512,768]{1,0:T(8,128)(2,1)S(1)} %all_gather.3), kind=kOutput, calls=%fused_computation.23 | convolution fusion | flops 3229609984 | bytes 15484928 | tf_op jit(solution)/shard_map/dot_general | solution.py:12
  243.7 4.5 %exponential_reduce_fusion.1 = f32[4096]{0:T(1024)S(1)} fusion(f32[4096,512]{0,1:T(8,128)} %get-tuple-element.9, f32[4096]{0:T(1024)S(1)} %get-tuple-element.8), kind=kLoop, calls=%fused_computation.6 | loop fusion | flops 4190208 | bytes 8421376 | tf_op jit(solution)/shard_map/reduce_sum | solution.py:54
  248.4 0.7 reshape.58
  249.1 9.0 %all-to-all-start.1 = ((f32[64,1,128]{2,1,0:T(1,128)}), f32[64,1,128]{2,1,0:T(1,128)S(1)}, u32[]{:S(2)}, u32[]{:S(2)}) async-start(f32[64,1,128]{2,1,0:T(1,128)} %reshape.58), calls=%async_computation.1 | async-start | bytes 65536 | tf_op jit(solution)/shard_map/all_to_all | solution.py:24
  258.1 8.5 %fusion.5 = (f32[4096]{0:T(1024)S(1)}, f32[4096,512]{0,1:T(8,128)}) fusion(f32[512]{0:T(512)S(1)} %multiply_reduce_fusion, bf16[4096,768]{1,0:T(8,128)(2,1)} %bitcast.18, bf16[512,768]{1,0:T(8,128)(2,1)S(1)} %all_gather.3), kind=kOutput, calls=%fused_computation.24 | convolution fusion | flops 3229609984 | bytes 15484928 | tf_op jit(solution)/shard_map/dot_general | solution.py:12
  266.7 4.5 %exponential_reduce_fusion = f32[4096]{0:T(1024)S(1)} fusion(f32[4096,512]{0,1:T(8,128)} %get-tuple-element.11, f32[4096]{0:T(1024)S(1)} %get-tuple-element.10), kind=kLoop, calls=%fused_computation.3 | loop fusion | flops 4190208 | bytes 8421376 | tf_op jit(solution)/shard_map/reduce_sum | solution.py:54
  272.1 9.8 %all-to-all-start.3 = ((f32[64,1,128]{2,1,0:T(1,128)}), f32[64,1,128]{2,1,0:T(1,128)S(1)}, u32[]{:S(2)}, u32[]{:S(2)}) async-start(f32[64,1,128]{2,1,0:T(1,128)} %reshape.60), calls=%async_computation.3 | async-start | bytes 65536 | tf_op jit(solution)/shard_map/all_to_all | solution.py:24
  283.4 7.0 %all-to-all-done.3 = f32[64,1,128]{2,1,0:T(1,128)S(1)} async-done(((f32[64,1,128]{2,1,0:T(1,128)}), f32[64,1,128]{2,1,0:T(1,128)S(1)}, u32[]{:S(2)}, u32[]{:S(2)}) %all-to-all-start.3) | async-done | bytes 32800 | tf_op jit(solution)/shard_map/all_to_all | solution.py:24
  291.0 4.7 %all-to-all-start.2 = ((f32[64,1,64]{2,1,0:T(1,128)}), f32[64,1,64]{2,1,0:T(1,128)S(1)}, u32[]{:S(2)}, u32[]{:S(2)}) async-start(f32[64,1,64]{2,1,0:T(1,128)} %broadcast_in_dim.4), calls=%async_computation.2 | async-start | bytes 65536 | tf_op jit(solution)/shard_map/all_to_all | solution.py:30
  296.6 7.4 %all-to-all-done.2 = f32[64,1,64]{2,1,0:T(1,128)S(1)} async-done(((f32[64,1,64]{2,1,0:T(1,128)}), f32[64,1,64]{2,1,0:T(1,128)S(1)}, u32[]{:S(2)}, u32[]{:S(2)}) %all-to-all-start.2) | async-done | bytes 16416 | tf_op jit(solution)/shard_map/all_to_all | solution.py:30
  304.7 4.9 %all-to-all-start.4 = ((f32[64,1,64]{2,1,0:T(1,128)}), f32[64,1,64]{2,1,0:T(1,128)S(1)}, u32[]{:S(2)}, u32[]{:S(2)}) async-start(f32[64,1,64]{2,1,0:T(1,128)} %broadcast_in_dim.5), calls=%async_computation.4 | async-start | bytes 65536 | tf_op jit(solution)/shard_map/all_to_all | solution.py:30
  310.1 0.7 reduce.8
  310.9 7.7 %fusion = f32[512,768]{1,0:T(8,128)S(1)} fusion(bf16[4096,768]{1,0:T(8,128)(2,1)} %bitcast.21, f32[4096,512]{0,1:T(8,128)} %get-tuple-element.9, f32[4096]{0:T(1024)S(1)} %sub.72), kind=kOutput, calls=%fused_computation.10 | convolution fusion | flops 3225419776 | bytes 16269312 | tf_op jit(solution)/shard_map/dot_general | solution.py:58
  318.6 0.7 reduce.9
  319.4 9.8 %convolution_add_fusion = f32[512,768]{1,0:T(8,128)} fusion(f32[512,768]{1,0:T(8,128)S(1)} %fusion, bf16[4096,768]{1,0:T(8,128)(2,1)} %bitcast.19, f32[4096,512]{0,1:T(8,128)} %get-tuple-element.11, f32[4096]{0:T(1024)S(1)} %sub.80), kind=kOutput, calls=%fused_computation.9 | convolution fusion | flops 3225812992 | bytes 17842176 | tf_op jit(solution)/shard_map/dot_general | solution.py:58
  331.1 7.1 %convert_reduce_fusion = (f32[512]{0:T(512)S(1)}, f32[512]{0:T(512)S(1)}) fusion(f32[4096,512]{0,1:T(8,128)} %get-tuple-element.11, f32[4096]{0:T(1024)S(1)} %sub.80, f32[4096,512]{0,1:T(8,128)} %get-tuple-element.9, f32[4096]{0:T(1024)S(1)} %sub.72), kind=kLoop, calls=%fused_computation | loop fusion | flops 16776192 | bytes 16814080 | tf_op jit(solution)/shard_map/reduce_sum | solution.py:61
  338.1 7.7 %all-reduce = f32[512]{0:T(512)S(1)} all-reduce(f32[512]{0:T(512)S(1)} %add.38), channel_id=3, replica_groups=mesh['dp'=2,'cent'=64] {'dp'}, use_global_device_ids=true, to_apply=%region_12.0.clone | all-reduce | flops 512 | bytes 4096
  345.9 1.3 reduce-scatter.2.cloned.1.call-done
  347.2 2.1 add_divide_fusion
  (41 shorter events, 7.1 us)
Async XLA Ops:
  14.1 12.3 %copy-start.1 = (f32[256,768]{1,0:T(8,128)S(1)}, f32[256,768]{1,0:T(8,128)}, u32[]{:S(2)}) copy-start(f32[256,768]{1,0:T(8,128)} %param.3) | copy-start | bytes 2359300
  14.1 215.1 %all-to-all-start = ((bf16[64,128,768]{2,1,0:T(8,128)(2,1)}), bf16[64,128,768]{2,1,0:T(8,128)(2,1)}, u32[]{:S(2)}, u32[]{:S(2)}) async-start(bf16[64,128,768]{2,1,0:T(8,128)(2,1)} %stack.6), calls=%async_computation | async-start | bytes 25165824 | tf_op jit(solution)/shard_map/all_to_all | solution.py:42
  237.8 5.8 %copy-start = (bf16[64,1,64,768]{3,2,1,0:T(8,128)(2,1)}, bf16[64,1,64,768]{3,2,1,0:T(8,128)(2,1)S(1)}, u32[]{:S(2)}) copy-start(bf16[64,1,64,768]{3,2,1,0:T(8,128)(2,1)S(1)} %get-tuple-element.3) | copy-start | bytes 18874372
  249.1 23.0 %all-to-all-start.1 = ((f32[64,1,128]{2,1,0:T(1,128)}), f32[64,1,128]{2,1,0:T(1,128)S(1)}, u32[]{:S(2)}, u32[]{:S(2)}) async-start(f32[64,1,128]{2,1,0:T(1,128)} %reshape.58), calls=%async_computation.1 | async-start | bytes 65536 | tf_op jit(solution)/shard_map/all_to_all | solution.py:24
  272.1 18.2 %all-to-all-start.3 = ((f32[64,1,128]{2,1,0:T(1,128)}), f32[64,1,128]{2,1,0:T(1,128)S(1)}, u32[]{:S(2)}, u32[]{:S(2)}) async-start(f32[64,1,128]{2,1,0:T(1,128)} %reshape.60), calls=%async_computation.3 | async-start | bytes 65536 | tf_op jit(solution)/shard_map/all_to_all | solution.py:24
  291.0 13.0 %all-to-all-start.2 = ((f32[64,1,64]{2,1,0:T(1,128)}), f32[64,1,64]{2,1,0:T(1,128)S(1)}, u32[]{:S(2)}, u32[]{:S(2)}) async-start(f32[64,1,64]{2,1,0:T(1,128)} %broadcast_in_dim.4), calls=%async_computation.2 | async-start | bytes 65536 | tf_op jit(solution)/shard_map/all_to_all | solution.py:30
  304.7 14.0 %all-to-all-start.4 = ((f32[64,1,64]{2,1,0:T(1,128)}), f32[64,1,64]{2,1,0:T(1,128)S(1)}, u32[]{:S(2)}, u32[]{:S(2)}) async-start(f32[64,1,64]{2,1,0:T(1,128)} %broadcast_in_dim.5), calls=%async_computation.4 | async-start | bytes 65536 | tf_op jit(solution)/shard_map/all_to_all | solution.py:30
  309.5 37.7 %reduce-scatter.2.cloned.1.call-start = ((), (), s32[]{:S(2)}) async-start(), calls=%async_computation.6 | async-start | bytes 2359296 | tf_op jit(solution)/shard_map/reduce_scatter | solution.py:64
  319.4 9.8 %copy-start.2 = (u32[128]{0:T(128)S(1)}, u32[128]{0:T(128)}, u32[]{:S(2)}) copy-start(u32[128]{0:T(128)} %constant.12) | copy-start | bytes 1540
Sparse Core Ops, SparseCore 0:
  329.3 17.8 reduce-scatter.1
